TPU v7x, 512 devices: a whole 4x8x8 slice. The times are simulated.
512 devices in a mesh: dp: 4 (over y_lo, core), seq: 4 (over x), fsdp: 32 (over y_hi, z).
Axes of the slice: x: 4, y: 8 (y_hi: 4, y_lo: 2; y = y_hi * 2 + y_lo), z: 8, core: 2. Of those that a mesh axis runs over, the one named last changes fastest.
Arguments:
- patches: bfloat16 [128, 768, 6144], P(('dp', 'fsdp'), 'seq'), may hold values from -100 to 100
- segments: int32 [128, 768], P(('dp', 'fsdp'), 'seq'), may hold values from 0 to 7, never falling along the last dimension, each value on 1 to 384 neighbouring positions
- qkv_weight: bfloat16 [6144, 384], P('fsdp'), may hold values from -0.078125 to 0.078125
- cotangent: bfloat16 [128, 768, 128], P(('dp', 'fsdp'), 'seq'), may hold values from -6 to 6
Outputs:
- input_grad: bfloat16 [128, 768, 6144], P(('dp', 'fsdp'), 'seq')
- weight_grad: float32 [6144, 384], P('fsdp')
Inputs may be any that keep to these rules, and one draw needn't show every extreme that they name: `segments`: within a sequence the image number never falls; each of the 8 images has 1 to 384 patches and one has exactly 384.
All inputs are finite; a program needn't handle non-finite values.
Results may differ from a plain program's by a relative error of at most 0.034.
The roundings to bfloat16 on the way count: a program that leaves them out, or rounds other values in their place, can miss the bound.
Values may be sent and summed in bfloat16 or wider, within the bound.
No kernel may reach another device: no remote copies, remote signals or barrier semaphores. Data moves between devices by JAX's collectives and lax.ppermute only.
A program may use at most 64 MiB of HBM per device.

v0:
```python
import functools
import jax
import jax.numpy as jnp
from jax import lax
from jax.sharding import PartitionSpec as P


def contract_first(left, right):
    return lax.dot_general(
        left, right, (((0,), (0,)), ((), ())), preferred_element_type=jnp.float32
    )


def contract_last(left, right):
    return lax.dot_general(
        left, right, (((1,), (1,)), ((), ())), preferred_element_type=jnp.float32
    )


def dp_partner(x, bit):
    pairs = [(i, i ^ bit) for i in range(lax.axis_size("dp"))]
    return lax.ppermute(x, "dp", perm=pairs)


class Ring:

    def __init__(self, axis, size, inner):
        self.axis, self.size, self.inner = (axis, size, inner)

    def total(self):
        return lax.axis_size(self.axis)

    def position(self):
        return lax.axis_index(self.axis) // self.inner % self.size

    def shift(self, x, step):
        n, inner, total = (self.size, self.inner, self.total())
        pairs = []
        for i in range(total):
            pos = i // inner % n
            base = i - pos * inner
            pairs.append((i, base + (pos + step) % n * inner))
        return lax.ppermute(x, self.axis, perm=pairs)


def ring_gather(x, ring, beside=None, late=None):
    n = ring.size
    got, slot = ([x], {0: 0})
    cw, ccw = (x, x)
    last_cw = n - 1 if (n - 1) % 2 == 1 else n - 2
    last_ccw = n - 1 if (n - 1) % 2 == 0 else n - 2
    for t in range(1, n):
        if t % 2 == 1:
            cw = ring.shift(cw, 1)
            if t == 1 and beside is not None:
                cw, beside = lax.optimization_barrier((cw, beside))
            if t == last_cw and late is not None:
                cw, late = lax.optimization_barrier((cw, late))
            slot[(n - (t + 1) // 2) % n] = len(got)
            got.append(cw)
        else:
            ccw = ring.shift(ccw, -1)
            if t == last_ccw and late is not None:
                value, make = late
                ccw, value = lax.optimization_barrier((ccw, value))
                late = make(value)
            slot[t // 2] = len(got)
            got.append(ccw)
    if late is not None:
        return (jnp.stack(got), [slot[k] for k in range(n)], late)
    return (jnp.stack(got), [slot[k] for k in range(n)], beside)


def ring_reduce_scatter(blocks, ring, axis=0, beside=None):
    n = ring.size
    me = ring.position()

    def pick(index):
        return lax.dynamic_index_in_dim(blocks, index % n, axis=axis, keepdims=False)

    total = pick(me)
    if n == 1:
        return (total, beside)
    up, down = (n // 2, (n - 1) // 2)
    acc = pick(me + up)
    for t in range(1, up + 1):
        acc = ring.shift(acc.astype(jnp.bfloat16), 1)
        if t == 1 and beside is not None:
            acc, beside = lax.optimization_barrier((acc, beside))
        acc = acc.astype(jnp.float32)
        if t < up:
            acc = acc + pick(me + up - t)
    total = total + acc
    if down:
        acc = pick(me - down)
        for t in range(1, down + 1):
            acc = ring.shift(acc.astype(jnp.bfloat16), -1).astype(jnp.float32)
            if t < down:
                acc = acc + pick(me - down + t)
        total = total + acc
    return (total, beside)


def shards(patches, segments, qkv_weight, cotangent, inner_fsdp):
    features = patches[0]
    image_ids = segments[0]
    grad_out = cotangent[0]
    width_head = cotangent.shape[2]
    width_all = qkv_weight.shape[1]
    rows_w = qkv_weight.shape[0]
    half = width_all // 2
    scale = width_head ** (-0.5)
    core = lax.axis_index("dp") % 2
    first = core == 0
    outer_fsdp = lax.axis_size("fh")
    n_fsdp = outer_fsdp * inner_fsdp
    ring_y = Ring("fh", outer_fsdp, 1)
    ring_z = Ring("fz", inner_fsdp, 1)
    ring_x = Ring("seq", lax.axis_size("seq"), 1)
    w_mine = lax.dynamic_slice_in_dim(qkv_weight, core * half, half, axis=1)
    stack_y = lax.all_gather(w_mine, "fh", axis=0, tiled=False)
    relayout = lambda f: f.reshape(f.shape[0], outer_fsdp, inner_fsdp, rows_w)
    stack_zy, slot_z, blocked = ring_gather(stack_y, ring_z, late=(features, relayout))
    flat = stack_zy.reshape(-1, rows_w, half)
    me_y, me_z = (ring_y.position(), ring_z.position())
    absolute = jnp.arange(n_fsdp, dtype=jnp.int32)
    rel_z = (absolute % inner_fsdp - me_z) % inner_fsdp
    order = jnp.asarray(slot_z, jnp.int32)[rel_z] * outer_fsdp + absolute // inner_fsdp
    w_mine_all = jnp.take(flat, order, axis=0, mode="clip").reshape(n_fsdp * rows_w, half)
    w_other_all = dp_partner(w_mine_all, 1)
    h_mine = jnp.dot(features, w_mine_all, preferred_element_type=jnp.float32)
    h_other = jnp.dot(features, w_other_all, preferred_element_type=jnp.float32)
    projected = jnp.where(
        first,
        jnp.concatenate([h_mine, h_other], axis=1),
        jnp.concatenate([h_other, h_mine], axis=1),
    )
    heads = projected.astype(jnp.bfloat16)
    n_rows = features.shape[0]
    n_x = ring_x.size
    me_x = ring_x.position()
    ids_col = jnp.broadcast_to(image_ids.astype(jnp.bfloat16)[:, None], (n_rows, width_head))
    packed = jnp.concatenate([heads, grad_out, ids_col], axis=1)
    packed_all = lax.all_gather(packed, "seq", axis=0, tiled=True)
    query_all = packed_all[:, :width_head]
    keys_all = packed_all[:, width_head : 2 * width_head]
    values_all = packed_all[:, 2 * width_head : 3 * width_head]
    grad_out_all = packed_all[:, 3 * width_head : 4 * width_head]
    images_all = packed_all[:, 4 * width_head]
    scores = contract_last(query_all, keys_all) * scale
    allowed = images_all[:, None] == images_all[None, :]
    highest = jnp.max(jnp.where(allowed, scores, -jnp.inf), axis=1)
    summed = jnp.sum(jnp.where(allowed, jnp.exp(scores - highest[:, None]), 0.0), axis=1)
    log_total = highest + jnp.log(summed)
    attention = jnp.where(allowed, jnp.exp(scores - log_total[:, None]), 0.0)
    attention_low = attention.astype(jnp.bfloat16)
    output = jnp.dot(attention_low, values_all, preferred_element_type=jnp.float32)
    delta_rows = jnp.sum(grad_out_all.astype(jnp.float32) * output, axis=1)
    grad_attention = contract_last(grad_out_all, values_all)
    grad_scores = (attention * (grad_attention - delta_rows[:, None]) * scale).astype(jnp.bfloat16)
    start = me_x * n_rows
    own_rows = lax.dynamic_slice_in_dim(grad_scores, start, n_rows, axis=0)
    own_cols = lax.dynamic_slice_in_dim(grad_scores, start, n_rows, axis=1)
    own_attention = lax.dynamic_slice_in_dim(attention_low, start, n_rows, axis=1)
    grad_query = jnp.dot(own_rows, keys_all, preferred_element_type=jnp.float32)
    grad_key = contract_first(own_cols, query_all)
    grad_value = contract_first(own_attention, grad_out_all)
    grad_heads = jnp.concatenate([grad_query, grad_key, grad_value], axis=1).astype(jnp.bfloat16)
    g_lo = grad_heads[:, :half]
    g_hi = grad_heads[:, half:]
    g_mine = jnp.where(first, g_lo, g_hi)
    g_other = jnp.where(first, g_hi, g_lo)
    input_grad = (contract_last(g_mine, w_mine_all) + contract_last(g_other, w_other_all)).astype(
        jnp.bfloat16
    )
    wg_other = jnp.einsum("pyzd,pc->zydc", blocked, g_other, preferred_element_type=jnp.float32)
    wg_from_partner = dp_partner(wg_other.astype(jnp.bfloat16), 1)
    wg_mine = jnp.einsum("pyzd,pc->zydc", blocked, g_mine, preferred_element_type=jnp.float32)
    wg_mine, wg_from_partner = lax.optimization_barrier((wg_mine, wg_from_partner))
    blocks = wg_mine + wg_from_partner.astype(jnp.float32)
    over_z, input_grad = ring_reduce_scatter(blocks, ring_z, axis=0, beside=input_grad)
    over_fsdp, _ = ring_reduce_scatter(over_z, ring_y)
    by_seq = lax.all_gather(over_fsdp, "seq", axis=0, tiled=False)
    over_seq = by_seq[0]
    for s_i in range(1, by_seq.shape[0]):
        over_seq = over_seq + by_seq[s_i]
    by_dp = lax.all_gather(over_seq, "dp", axis=0, tiled=False)
    halves = []
    for c in range(2):
        part = by_dp[c]
        for d in range(c + 2, by_dp.shape[0], 2):
            part = part + by_dp[d]
        halves.append(part)
    weight_grad = jnp.concatenate(halves, axis=1)
    return (input_grad[None], weight_grad)


def inner_ring_size(mesh):
    axis = mesh.axis_names.index("fsdp")
    line = mesh.devices[tuple((0 if a != axis else slice(None) for a in range(mesh.devices.ndim)))]
    line = list(line)
    if not hasattr(line[0], "coords"):
        return len(line)
    count = 1
    while count < len(line) and line[count].coords[1] == line[0].coords[1]:
        count += 1
    return count


def solution(mesh):
    inner = inner_ring_size(mesh)
    sizes = dict(zip(mesh.axis_names, mesh.devices.shape))
    split = jax.sharding.Mesh(
        mesh.devices.reshape(sizes["dp"], sizes["seq"], sizes["fsdp"] // inner, inner),
        ("dp", "seq", "fh", "fz"),
    )
    rows = ("dp", "fh", "fz")
    placed = (P(rows, "seq", None), P(rows, "seq"), P(("fh", "fz"), None), P(rows, "seq", None))
    return jax.shard_map(
        functools.partial(shards, inner_fsdp=inner),
        mesh=split,
        in_specs=placed,
        out_specs=(P(rows, "seq", None), P(("fh", "fz"), None)),
        check_vma=False,
    )
```

profile of v0, /device:TPU:75, one launch (start us, length us, event | category | flops | bytes accessed | tf_op | source)
XLA Modules:
  0.0 222.7 jit_solution(9267431359710863556)
XLA Ops:
  0.7 0.9 copy-done
  1.6 13.7 %all-gather = bf16[768,192]{1,0:T(8,128)(2,1)S(1)} all-gather(bf16[192,192]{1,0:T(8,128)(2,1)S(1)} %constant_dynamic-slice_fusion), channel_id=2, replica_groups=mesh['dp'=4,'seq'=4,'fh'=4,'fz'=8] {'fh'}, dimensions={0}, use_global_device_ids=true | all-gather | bytes 368640 | tf_op jit(solution)/shard_map/all_gather | solution.py:121
  15.3 4.0 %collective-permute-start = (bf16[4,192,192]{2,1,0:T(8,128)(2,1)S(1)}, bf16[4,192,192]{2,1,0:T(8,128)(2,1)}, u32[]{:S(2)}, u32[]{:S(2)}) collective-permute-start(bf16[4,192,192]{2,1,0:T(8,128)(2,1)S(1)} %bitcast.108), channel_id=1, source_target_pairs={{0,1},{1,2},{2,3},{3,4},{4,5},{5,6},{6,7},{7,0},{8,9},{9,10},{10,1... | collective-permute-start | bytes 884744 | tf_op jit(solution)/shard_map/ppermute | solution.py:43
  19.3 1.9 collective-permute-start.1
  21.3 0.8 constant_dynamic-update-slice_fusion
  22.1 1.5 gather_fusion
  24.0 4.0 %collective-permute-start.2 = (bf16[4,192,192]{2,1,0:T(8,128)(2,1)}, bf16[4,192,192]{2,1,0:T(8,128)(2,1)S(1)}, u32[]{:S(2)}, u32[]{:S(2)}) collective-permute-start(bf16[4,192,192]{2,1,0:T(8,128)(2,1)} %collective-permute-done), channel_id=1, source_target_pairs={{0,1},{1,2},{2,3},{3,4},{4,5},{5,6},{6,7},{7,0},{8,9},{9,10},{10,1... | collective-permute-start | bytes 884744 | tf_op jit(solution)/shard_map/ppermute | solution.py:43
  28.0 1.8 bitcast_dynamic-update-slice_fusion.6
  29.8 6.4 %collective-permute-start.3 = (bf16[4,192,192]{2,1,0:T(8,128)(2,1)S(1)}, bf16[4,192,192]{2,1,0:T(8,128)(2,1)S(1)}, u32[]{:S(2)}, u32[]{:S(2)}) collective-permute-start(bf16[4,192,192]{2,1,0:T(8,128)(2,1)S(1)} %collective-permute-done.1), channel_id=1, source_target_pairs={{0,7},{1,0},{2,1},{3,2},{4,3},{5,4},{6,5},{7,6},{8,15},{9,8},{10,9... | collective-permute-start | bytes 884744 | tf_op jit(solution)/shard_map/ppermute | solution.py:43
  36.2 0.8 bitcast_dynamic-update-slice_fusion.5
  37.0 0.9 collective-permute-done.2
  37.9 1.9 collective-permute-start.4
  39.8 0.8 bitcast_dynamic-update-slice_fusion.4
  40.9 4.6 %collective-permute-start.5 = (bf16[4,192,192]{2,1,0:T(8,128)(2,1)S(1)}, bf16[4,192,192]{2,1,0:T(8,128)(2,1)S(1)}, u32[]{:S(2)}, u32[]{:S(2)}) collective-permute-start(bf16[4,192,192]{2,1,0:T(8,128)(2,1)S(1)} %collective-permute-done.3), channel_id=1, source_target_pairs={{0,7},{1,0},{2,1},{3,2},{4,3},{5,4},{6,5},{7,6},{8,15},{9,8},{10,9... | collective-permute-start | bytes 884744 | tf_op jit(solution)/shard_map/ppermute | solution.py:43
  45.5 0.8 bitcast_dynamic-update-slice_fusion.3
  46.3 1.4 collective-permute-done.4
  47.7 1.9 collective-permute-start.6
  49.6 1.8 bitcast_dynamic-update-slice_fusion.2
  51.5 4.5 %reshape.141 = bf16[192,4,8,192]{3,2,1,0:T(8,128)(2,1)} reshape(bf16[192,6144]{1,0:T(8,128)(2,1)S(1)} %bitcast.105) | data formatting | bytes 4718592 | tf_op jit(solution)/shard_map/reshape | solution.py:122
  56.0 0.8 bitcast_dynamic-update-slice_fusion.1
  56.8 1.4 collective-permute-done.6
  58.2 1.8 bitcast_dynamic-update-slice_fusion
  60.0 2.6 %gather_fusion.1 = bf16[32,192,192]{2,1,0:T(8,128)(2,1)S(1)} fusion(bf16[32,192,192]{2,1,0:T(8,128)(2,1)} %bitcast.106, s32[1024]{0:T(1024)S(1)} %pad_clamp_fusion), kind=kCustom, calls=%fused_computation.1 | custom fusion | bytes 4718720 | tf_op jit(solution)/shard_map/jit(_take)/gather | solution.py:129
  62.6 2.6 %copy.31 = bf16[6144,192]{0,1:T(8,128)(2,1)} copy(bf16[6144,192]{1,0:T(8,128)(2,1)S(1)} %bitcast.102) | data formatting | bytes 4718592 | tf_op jit(solution)/shard_map/reshape | solution.py:129
  65.2 10.2 %collective-permute-start.7 = (bf16[6144,192]{0,1:T(8,128)(2,1)}, bf16[6144,192]{0,1:T(8,128)(2,1)}, u32[]{:S(2)}, u32[]{:S(2)}) collective-permute-start(bf16[6144,192]{0,1:T(8,128)(2,1)} %copy.31), channel_id=1, source_target_pairs={{0,128},{128,0},{256,384},{384,256},{1,129},{129,1},{257,385},{385... | collective-permute-start | bytes 7077896 | tf_op jit(solution)/shard_map/ppermute | solution.py:22
  75.5 2.6 %convolution_bitcast_fusion.1 = bf16[192,192]{1,0:T(8,128)(2,1)S(1)} fusion(bf16[6144,192]{1,0:T(8,128)(2,1)S(1)} %bitcast.103, bf16[1,192,6144]{2,1,0:T(8,128)(2,1)} %param.5), kind=kOutput, calls=%fused_computation.21 | convolution fusion | flops 452984832 | bytes 4792320 | tf_op jit(solution)/shard_map/dot_general | solution.py:131
  78.1 1.8 collective-permute-done.7
  79.9 2.5 %convolution_bitcast_fusion = bf16[192,192]{1,0:T(8,128)(2,1)S(1)} fusion(bf16[6144,192]{0,1:T(8,128)(2,1)} %collective-permute-done.7, bf16[1,192,6144]{2,1,0:T(8,128)(2,1)S(1)} %copy-done.5), kind=kOutput, calls=%fused_computation.20 | convolution fusion | flops 452984832 | bytes 4792320 | tf_op jit(solution)/shard_map/dot_general | solution.py:132
  82.7 12.4 %all_gather.21 = bf16[768,640]{1,0:T(8,128)(2,1)S(1)} all-gather(bf16[192,640]{1,0:T(8,128)(2,1)S(1)} %pad_maximum_fusion.1), channel_id=1, replica_groups=mesh['dp'=4,'seq'=4,'fh'=4,'fz'=8] {'seq'}, dimensions={0}, use_global_device_ids=true | all-gather | bytes 1228800 | tf_op jit(solution)/shard_map/all_gather | solution.py:144
  95.7 0.6 fusion.9
  96.8 0.6 fusion.13
  97.6 0.8 multiply_convert_fusion
  99.5 4.1 %convert_bitcast_fusion = bf16[8,4,192,192]{2,3,0,1:T(8,128)(2,1)} fusion(bf16[192,4,8,192]{3,2,1,0:T(8,128)(2,1)S(1)} %copy-done.1, pred[]{:T(512)S(6)} %eq.39, bf16[192,128]{1,0:T(8,128)(2,1)S(1)} %convolution_convert_fusion.1, bf16[192,128]{1,0:T(8,128)(2,1)S(1)} %convolution_convert_fusion.2, bf16[192,128]{1,0:T(8,128)(2,1)S(1)} %convolution_convert_fusion), kind=kOutput, calls=%fused_computation.8 | convolution fusion | flops 454496256 | bytes 4866049 | tf_op jit(solution)/shard_map/pyzd,pc->zydc/dot_general | solution.py:176
  103.6 5.4 %collective-permute-start.8 = (bf16[8,4,192,192]{2,3,0,1:T(8,128)(2,1)}, bf16[8,4,192,192]{2,3,0,1:T(8,128)(2,1)}, u32[]{:S(2)}, u32[]{:S(2)}) collective-permute-start(bf16[8,4,192,192]{2,3,0,1:T(8,128)(2,1)} %convert_bitcast_fusion), channel_id=1, source_target_pairs={{0,128},{128,0},{256,384},{384,256},{1,129},{129,1},{257,385},{385... | collective-permute-start | bytes 7077896 | tf_op jit(solution)/shard_map/ppermute | solution.py:22
  109.1 1.2 fusion.54
  110.3 0.7 copy-done.2
  111.0 2.4 %fusion.5 = f32[8,4,192,192]{2,3,0,1:T(8,128)S(1)} fusion(bf16[192,4,8,192]{3,2,1,0:T(8,128)(2,1)S(1)} %copy-done.2, pred[]{:T(512)S(6)} %eq.39, bf16[192,128]{1,0:T(8,128)(2,1)S(1)} %convolution_convert_fusion.1, bf16[192,128]{1,0:T(8,128)(2,1)S(1)} %convolution_convert_fusion.2, bf16[192,128]{1,0:T(8,128)(2,1)S(1)} %convolution_convert_fusion), kind=kOutput, calls=%fused_computation.13 | convolution fusion | flops 453316608 | bytes 7225345 | tf_op jit(solution)/shard_map/pyzd,pc->zydc/dot_general | solution.py:178
  113.4 1.1 collective-permute-done.8
  114.5 3.0 %convert_add_fusion = f32[8,4,192,192]{2,3,0,1:T(8,128)S(1)} fusion(f32[8,4,192,192]{2,3,0,1:T(8,128)S(1)} %fusion.5, bf16[8,4,192,192]{2,3,0,1:T(8,128)(2,1)} %collective-permute-done.8), kind=kLoop, calls=%fused_computation.4 | loop fusion | flops 2359296 | bytes 11796480 | tf_op jit(solution)/shard_map/add | solution.py:180
  117.6 2.1 collective-permute-start.9
  119.7 3.9 %fusion = bf16[192,6144]{1,0:T(8,128)(2,1)} fusion(f32[192,6144]{1,0:T(8,128)S(1)} %fusion.54, bf16[6144,192]{0,1:T(8,128)(2,1)} %collective-permute-done.7, pred[]{:T(512)S(6)} %eq.39, bf16[192,128]{1,0:T(8,128)(2,1)S(1)} %convolution_convert_fusion.1, bf16[192,128]{1,0:T(8,128)(2,1)S(1)} %convolution_convert_fusion.2, ...), kind=kOutput, calls=%fused_computation.3 | convolution fusion | flops 455675904 | bytes 9584641 | tf_op jit(solution)/shard_map/dot_general | solution.py:15
  123.6 4.7 %collective-permute-start.13 = (bf16[4,192,192]{1,2,0:T(8,128)(2,1)S(1)}, bf16[4,192,192]{1,2,0:T(8,128)(2,1)S(1)}, u32[]{:S(2)}, u32[]{:S(2)}) collective-permute-start(bf16[4,192,192]{1,2,0:T(8,128)(2,1)S(1)} %get-tuple-element.26), channel_id=1, source_target_pairs={{0,7},{1,0},{2,1},{3,2},{4,3},{5,4},{6,5},{7,6},{8,15},{9,8},{10,9... | collective-permute-start | bytes 884744 | tf_op jit(solution)/shard_map/ppermute | solution.py:43
  128.4 3.3 %collective-permute-done.9 = bf16[4,192,192]{1,2,0:T(8,128)(2,1)S(1)} collective-permute-done((bf16[4,192,192]{1,2,0:T(8,128)(2,1)S(1)}, bf16[4,192,192]{1,2,0:T(8,128)(2,1)S(1)}, u32[]{:S(2)}, u32[]{:S(2)}) %collective-permute-start.9) | collective-permute-done | bytes 294944 | tf_op jit(solution)/shard_map/ppermute | solution.py:43
  131.8 1.9 collective-permute-start.10
  133.7 4.2 %collective-permute-done.13 = bf16[4,192,192]{1,2,0:T(8,128)(2,1)S(1)} collective-permute-done((bf16[4,192,192]{1,2,0:T(8,128)(2,1)S(1)}, bf16[4,192,192]{1,2,0:T(8,128)(2,1)S(1)}, u32[]{:S(2)}, u32[]{:S(2)}) %collective-permute-start.13) | collective-permute-done | bytes 294944 | tf_op jit(solution)/shard_map/ppermute | solution.py:43
  137.9 6.4 %collective-permute-done.10 = bf16[4,192,192]{1,2,0:T(8,128)(2,1)S(1)} collective-permute-done((bf16[4,192,192]{1,2,0:T(8,128)(2,1)S(1)}, bf16[4,192,192]{1,2,0:T(8,128)(2,1)S(1)}, u32[]{:S(2)}, u32[]{:S(2)}) %collective-permute-start.10) | collective-permute-done | bytes 294944 | tf_op jit(solution)/shard_map/ppermute | solution.py:43
  144.3 1.6 fusion.17
  145.8 1.9 collective-permute-start.11
  147.7 4.3 %collective-permute-start.14 = (bf16[4,192,192]{1,2,0:T(8,128)(2,1)S(1)}, bf16[4,192,192]{1,2,0:T(8,128)(2,1)S(1)}, u32[]{:S(2)}, u32[]{:S(2)}) collective-permute-start(bf16[4,192,192]{1,2,0:T(8,128)(2,1)S(1)} %get-tuple-element.25), channel_id=1, source_target_pairs={{0,7},{1,0},{2,1},{3,2},{4,3},{5,4},{6,5},{7,6},{8,15},{9,8},{10,9... | collective-permute-start | bytes 884744 | tf_op jit(solution)/shard_map/ppermute | solution.py:43
  152.1 5.3 %collective-permute-done.11 = bf16[4,192,192]{1,2,0:T(8,128)(2,1)S(1)} collective-permute-done((bf16[4,192,192]{1,2,0:T(8,128)(2,1)S(1)}, bf16[4,192,192]{1,2,0:T(8,128)(2,1)S(1)}, u32[]{:S(2)}, u32[]{:S(2)}) %collective-permute-start.11) | collective-permute-done | bytes 294944 | tf_op jit(solution)/shard_map/ppermute | solution.py:43
  157.4 0.9 collective-permute-done.14
  158.3 1.6 fusion.16
  159.8 5.2 %collective-permute-start.12 = (bf16[4,192,192]{1,2,0:T(8,128)(2,1)S(1)}, bf16[4,192,192]{1,2,0:T(8,128)(2,1)S(1)}, u32[]{:S(2)}, u32[]{:S(2)}) collective-permute-start(bf16[4,192,192]{1,2,0:T(8,128)(2,1)S(1)} %get-tuple-element.22), channel_id=1, source_target_pairs={{0,1},{1,2},{2,3},{3,4},{4,5},{5,6},{6,7},{7,0},{8,9},{9,10},{10,1... | collective-permute-start | bytes 884744 | tf_op jit(solution)/shard_map/ppermute | solution.py:43
  165.1 1.9 collective-permute-start.15
  167.1 3.3 %collective-permute-done.12 = bf16[4,192,192]{1,2,0:T(8,128)(2,1)S(1)} collective-permute-done((bf16[4,192,192]{1,2,0:T(8,128)(2,1)S(1)}, bf16[4,192,192]{1,2,0:T(8,128)(2,1)S(1)}, u32[]{:S(2)}, u32[]{:S(2)}) %collective-permute-start.12) | collective-permute-done | bytes 294944 | tf_op jit(solution)/shard_map/ppermute | solution.py:43
  170.4 4.8 %collective-permute-done.15 = bf16[4,192,192]{1,2,0:T(8,128)(2,1)S(1)} collective-permute-done((bf16[4,192,192]{1,2,0:T(8,128)(2,1)S(1)}, bf16[4,192,192]{1,2,0:T(8,128)(2,1)S(1)}, u32[]{:S(2)}, u32[]{:S(2)}) %collective-permute-start.15) | collective-permute-done | bytes 294944 | tf_op jit(solution)/shard_map/ppermute | solution.py:43
  175.2 1.2 fusion.19
  176.5 2.7 %collective-permute-start.16 = (bf16[192,192]{0,1:T(8,128)(2,1)S(1)}, bf16[192,192]{0,1:T(8,128)(2,1)S(1)}, u32[]{:S(2)}, u32[]{:S(2)}) collective-permute-start(bf16[192,192]{0,1:T(8,128)(2,1)S(1)} %get-tuple-element.30), channel_id=1, source_target_pairs={{0,8},{8,16},{16,24},{24,0},{1,9},{9,17},{17,25},{25,1},{2,10},{10... | collective-permute-start | bytes 221192 | tf_op jit(solution)/shard_map/ppermute | solution.py:43
  179.3 4.7 %collective-permute-start.18 = (bf16[192,192]{0,1:T(8,128)(2,1)S(1)}, bf16[192,192]{0,1:T(8,128)(2,1)S(1)}, u32[]{:S(2)}, u32[]{:S(2)}) collective-permute-start(bf16[192,192]{0,1:T(8,128)(2,1)S(1)} %get-tuple-element.31), channel_id=1, source_target_pairs={{0,24},{8,0},{16,8},{24,16},{1,25},{9,1},{17,9},{25,17},{2,26},{10... | collective-permute-start | bytes 221192 | tf_op jit(solution)/shard_map/ppermute | solution.py:43
  184.0 1.9 collective-permute-start.17
  186.5 5.4 %collective-permute-done.17 = bf16[192,192]{0,1:T(8,128)(2,1)S(1)} collective-permute-done((bf16[192,192]{0,1:T(8,128)(2,1)S(1)}, bf16[192,192]{0,1:T(8,128)(2,1)S(1)}, u32[]{:S(2)}, u32[]{:S(2)}) %collective-permute-start.17) | collective-permute-done | bytes 73760 | tf_op jit(solution)/shard_map/ppermute | solution.py:43
  192.1 11.0 %all-gather.1 = f32[768,192]{1,0:T(8,128)S(1)} all-gather(f32[192,192]{1,0:T(8,128)S(1)} %copy.39), channel_id=3, replica_groups=mesh['dp'=4,'seq'=4,'fh'=4,'fz'=8] {'seq'}, dimensions={0}, use_global_device_ids=true | all-gather | bytes 737280 | tf_op jit(solution)/shard_map/all_gather | solution.py:183
  203.1 18.7 %all_gather.24 = f32[4,192,192]{2,1,0:T(8,128)S(1)} all-gather(f32[1,192,192]{2,1,0:T(8,128)S(1)} %fusion.28), channel_id=1, replica_groups=mesh['dp'=4,'seq'=4,'fh'=4,'fz'=8] {'dp'}, dimensions={0}, use_global_device_ids=true | all-gather | bytes 737280 | tf_op jit(solution)/shard_map/all_gather | solution.py:187
  221.9 0.8 pad_maximum_fusion
  (44 shorter events, 4.7 us)
Async XLA Ops:
  0.6 0.9 copy-start
  15.3 8.7 %collective-permute-start = (bf16[4,192,192]{2,1,0:T(8,128)(2,1)S(1)}, bf16[4,192,192]{2,1,0:T(8,128)(2,1)}, u32[]{:S(2)}, u32[]{:S(2)}) collective-permute-start(bf16[4,192,192]{2,1,0:T(8,128)(2,1)S(1)} %bitcast.108), channel_id=1, source_target_pairs={{0,1},{1,2},{2,3},{3,4},{4,5},{5,6},{6,7},{7,0},{8,9},{9,10},{10,1... | collective-permute-start | bytes 884744 | tf_op jit(solution)/shard_map/ppermute | solution.py:43
  19.3 10.5 %collective-permute-start.1 = (bf16[4,192,192]{2,1,0:T(8,128)(2,1)S(1)}, bf16[4,192,192]{2,1,0:T(8,128)(2,1)S(1)}, u32[]{:S(2)}, u32[]{:S(2)}) collective-permute-start(bf16[4,192,192]{2,1,0:T(8,128)(2,1)S(1)} %bitcast.109), channel_id=1, source_target_pairs={{0,7},{1,0},{2,1},{3,2},{4,3},{5,4},{6,5},{7,6},{8,15},{9,8},{10,9... | collective-permute-start | bytes 884744 | tf_op jit(solution)/shard_map/ppermute | solution.py:43
  22.1 29.4 %copy-start.4 = (bf16[1,192,6144]{2,1,0:T(8,128)(2,1)S(1)}, bf16[1,192,6144]{2,1,0:T(8,128)(2,1)}, u32[]{:S(2)}) copy-start(bf16[1,192,6144]{2,1,0:T(8,128)(2,1)} %param.5) | copy-start | bytes 7077892
  24.0 13.9 %collective-permute-start.2 = (bf16[4,192,192]{2,1,0:T(8,128)(2,1)}, bf16[4,192,192]{2,1,0:T(8,128)(2,1)S(1)}, u32[]{:S(2)}, u32[]{:S(2)}) collective-permute-start(bf16[4,192,192]{2,1,0:T(8,128)(2,1)} %collective-permute-done), channel_id=1, source_target_pairs={{0,1},{1,2},{2,3},{3,4},{4,5},{5,6},{6,7},{7,0},{8,9},{9,10},{10,1... | collective-permute-start | bytes 884744 | tf_op jit(solution)/shard_map/ppermute | solution.py:43
  29.8 11.1 %collective-permute-start.3 = (bf16[4,192,192]{2,1,0:T(8,128)(2,1)S(1)}, bf16[4,192,192]{2,1,0:T(8,128)(2,1)S(1)}, u32[]{:S(2)}, u32[]{:S(2)}) collective-permute-start(bf16[4,192,192]{2,1,0:T(8,128)(2,1)S(1)} %collective-permute-done.1), channel_id=1, source_target_pairs={{0,7},{1,0},{2,1},{3,2},{4,3},{5,4},{6,5},{7,6},{8,15},{9,8},{10,9... | collective-permute-start | bytes 884744 | tf_op jit(solution)/shard_map/ppermute | solution.py:43
  37.9 9.8 %collective-permute-start.4 = (bf16[4,192,192]{2,1,0:T(8,128)(2,1)S(1)}, bf16[4,192,192]{2,1,0:T(8,128)(2,1)}, u32[]{:S(2)}, u32[]{:S(2)}) collective-permute-start(bf16[4,192,192]{2,1,0:T(8,128)(2,1)S(1)} %collective-permute-done.2), channel_id=1, source_target_pairs={{0,1},{1,2},{2,3},{3,4},{4,5},{5,6},{6,7},{7,0},{8,9},{9,10},{10,1... | collective-permute-start | bytes 884744 | tf_op jit(solution)/shard_map/ppermute | solution.py:43
  40.9 10.5 %collective-permute-start.5 = (bf16[4,192,192]{2,1,0:T(8,128)(2,1)S(1)}, bf16[4,192,192]{2,1,0:T(8,128)(2,1)S(1)}, u32[]{:S(2)}, u32[]{:S(2)}) collective-permute-start(bf16[4,192,192]{2,1,0:T(8,128)(2,1)S(1)} %collective-permute-done.3), channel_id=1, source_target_pairs={{0,7},{1,0},{2,1},{3,2},{4,3},{5,4},{6,5},{7,6},{8,15},{9,8},{10,9... | collective-permute-start | bytes 884744 | tf_op jit(solution)/shard_map/ppermute | solution.py:43
  47.7 10.5 %collective-permute-start.6 = (bf16[4,192,192]{2,1,0:T(8,128)(2,1)}, bf16[4,192,192]{2,1,0:T(8,128)(2,1)}, u32[]{:S(2)}, u32[]{:S(2)}) collective-permute-start(bf16[4,192,192]{2,1,0:T(8,128)(2,1)} %collective-permute-done.4), channel_id=1, source_target_pairs={{0,1},{1,2},{2,3},{3,4},{4,5},{5,6},{6,7},{7,0},{8,9},{9,10},{10,1... | collective-permute-start | bytes 884744 | tf_op jit(solution)/shard_map/ppermute | solution.py:43
  62.6 12.8 %copy-start.7 = (s32[1,192]{1,0:T(1,128)S(1)}, s32[1,192]{1,0:T(1,128)}, u32[]{:S(2)}) copy-start(s32[1,192]{1,0:T(1,128)} %param.6) | copy-start | bytes 2308
  65.2 14.7 %collective-permute-start.7 = (bf16[6144,192]{0,1:T(8,128)(2,1)}, bf16[6144,192]{0,1:T(8,128)(2,1)}, u32[]{:S(2)}, u32[]{:S(2)}) collective-permute-start(bf16[6144,192]{0,1:T(8,128)(2,1)} %copy.31), channel_id=1, source_target_pairs={{0,128},{128,0},{256,384},{384,256},{1,129},{129,1},{257,385},{385... | collective-permute-start | bytes 7077896 | tf_op jit(solution)/shard_map/ppermute | solution.py:22
  75.5 4.4 %copy-start.5 = (bf16[1,192,6144]{2,1,0:T(8,128)(2,1)S(1)}, bf16[1,192,6144]{2,1,0:T(8,128)(2,1)}, u32[]{:S(2)}) copy-start(bf16[1,192,6144]{2,1,0:T(8,128)(2,1)} %param.5) | copy-start | bytes 7077892
  78.1 4.5 %copy-start.6 = (bf16[1,192,128]{2,1,0:T(8,128)(2,1)S(1)}, bf16[1,192,128]{2,1,0:T(8,128)(2,1)}, u32[]{:S(2)}) copy-start(bf16[1,192,128]{2,1,0:T(8,128)(2,1)} %param.8) | copy-start | bytes 147460
  97.6 1.9 copy-start.1
  103.6 10.9 %collective-permute-start.8 = (bf16[8,4,192,192]{2,3,0,1:T(8,128)(2,1)}, bf16[8,4,192,192]{2,3,0,1:T(8,128)(2,1)}, u32[]{:S(2)}, u32[]{:S(2)}) collective-permute-start(bf16[8,4,192,192]{2,3,0,1:T(8,128)(2,1)} %convert_bitcast_fusion), channel_id=1, source_target_pairs={{0,128},{128,0},{256,384},{384,256},{1,129},{129,1},{257,385},{385... | collective-permute-start | bytes 7077896 | tf_op jit(solution)/shard_map/ppermute | solution.py:22
  109.1 1.9 copy-start.2
  117.5 14.1 %copy-start.3 = (f32[8,4,192,192]{2,3,0,1:T(8,128)}, f32[8,4,192,192]{2,3,0,1:T(8,128)S(1)}, u32[]{:S(2)}) copy-start(f32[8,4,192,192]{2,3,0,1:T(8,128)S(1)} %convert_add_fusion) | copy-start | bytes 14155780
  117.6 14.0 %collective-permute-start.9 = (bf16[4,192,192]{1,2,0:T(8,128)(2,1)S(1)}, bf16[4,192,192]{1,2,0:T(8,128)(2,1)S(1)}, u32[]{:S(2)}, u32[]{:S(2)}) collective-permute-start(bf16[4,192,192]{1,2,0:T(8,128)(2,1)S(1)} %get-tuple-element.27), channel_id=1, source_target_pairs={{0,1},{1,2},{2,3},{3,4},{4,5},{5,6},{6,7},{7,0},{8,9},{9,10},{10,1... | collective-permute-start | bytes 884744 | tf_op jit(solution)/shard_map/ppermute | solution.py:43
  123.6 14.3 %collective-permute-start.13 = (bf16[4,192,192]{1,2,0:T(8,128)(2,1)S(1)}, bf16[4,192,192]{1,2,0:T(8,128)(2,1)S(1)}, u32[]{:S(2)}, u32[]{:S(2)}) collective-permute-start(bf16[4,192,192]{1,2,0:T(8,128)(2,1)S(1)} %get-tuple-element.26), channel_id=1, source_target_pairs={{0,7},{1,0},{2,1},{3,2},{4,3},{5,4},{6,5},{7,6},{8,15},{9,8},{10,9... | collective-permute-start | bytes 884744 | tf_op jit(solution)/shard_map/ppermute | solution.py:43
  131.8 12.5 %collective-permute-start.10 = (bf16[4,192,192]{1,2,0:T(8,128)(2,1)S(1)}, bf16[4,192,192]{1,2,0:T(8,128)(2,1)S(1)}, u32[]{:S(2)}, u32[]{:S(2)}) collective-permute-start(bf16[4,192,192]{1,2,0:T(8,128)(2,1)S(1)} %fusion.18), channel_id=1, source_target_pairs={{0,1},{1,2},{2,3},{3,4},{4,5},{5,6},{6,7},{7,0},{8,9},{9,10},{10,1... | collective-permute-start | bytes 884744 | tf_op jit(solution)/shard_map/ppermute | solution.py:43
  145.8 11.6 %collective-permute-start.11 = (bf16[4,192,192]{1,2,0:T(8,128)(2,1)S(1)}, bf16[4,192,192]{1,2,0:T(8,128)(2,1)S(1)}, u32[]{:S(2)}, u32[]{:S(2)}) collective-permute-start(bf16[4,192,192]{1,2,0:T(8,128)(2,1)S(1)} %get-tuple-element.24), channel_id=1, source_target_pairs={{0,1},{1,2},{2,3},{3,4},{4,5},{5,6},{6,7},{7,0},{8,9},{9,10},{10,1... | collective-permute-start | bytes 884744 | tf_op jit(solution)/shard_map/ppermute | solution.py:43
  147.7 10.5 %collective-permute-start.14 = (bf16[4,192,192]{1,2,0:T(8,128)(2,1)S(1)}, bf16[4,192,192]{1,2,0:T(8,128)(2,1)S(1)}, u32[]{:S(2)}, u32[]{:S(2)}) collective-permute-start(bf16[4,192,192]{1,2,0:T(8,128)(2,1)S(1)} %get-tuple-element.25), channel_id=1, source_target_pairs={{0,7},{1,0},{2,1},{3,2},{4,3},{5,4},{6,5},{7,6},{8,15},{9,8},{10,9... | collective-permute-start | bytes 884744 | tf_op jit(solution)/shard_map/ppermute | solution.py:43
  159.8 10.6 %collective-permute-start.12 = (bf16[4,192,192]{1,2,0:T(8,128)(2,1)S(1)}, bf16[4,192,192]{1,2,0:T(8,128)(2,1)S(1)}, u32[]{:S(2)}, u32[]{:S(2)}) collective-permute-start(bf16[4,192,192]{1,2,0:T(8,128)(2,1)S(1)} %get-tuple-element.22), channel_id=1, source_target_pairs={{0,1},{1,2},{2,3},{3,4},{4,5},{5,6},{6,7},{7,0},{8,9},{9,10},{10,1... | collective-permute-start | bytes 884744 | tf_op jit(solution)/shard_map/ppermute | solution.py:43
  165.1 10.1 %collective-permute-start.15 = (bf16[4,192,192]{1,2,0:T(8,128)(2,1)S(1)}, bf16[4,192,192]{1,2,0:T(8,128)(2,1)S(1)}, u32[]{:S(2)}, u32[]{:S(2)}) collective-permute-start(bf16[4,192,192]{1,2,0:T(8,128)(2,1)S(1)} %get-tuple-element.23), channel_id=1, source_target_pairs={{0,7},{1,0},{2,1},{3,2},{4,3},{5,4},{6,5},{7,6},{8,15},{9,8},{10,9... | collective-permute-start | bytes 884744 | tf_op jit(solution)/shard_map/ppermute | solution.py:43
  176.5 7.5 %collective-permute-start.16 = (bf16[192,192]{0,1:T(8,128)(2,1)S(1)}, bf16[192,192]{0,1:T(8,128)(2,1)S(1)}, u32[]{:S(2)}, u32[]{:S(2)}) collective-permute-start(bf16[192,192]{0,1:T(8,128)(2,1)S(1)} %get-tuple-element.30), channel_id=1, source_target_pairs={{0,8},{8,16},{16,24},{24,0},{1,9},{9,17},{17,25},{25,1},{2,10},{10... | collective-permute-start | bytes 221192 | tf_op jit(solution)/shard_map/ppermute | solution.py:43
  179.3 7.2 %collective-permute-start.18 = (bf16[192,192]{0,1:T(8,128)(2,1)S(1)}, bf16[192,192]{0,1:T(8,128)(2,1)S(1)}, u32[]{:S(2)}, u32[]{:S(2)}) collective-permute-start(bf16[192,192]{0,1:T(8,128)(2,1)S(1)} %get-tuple-element.31), channel_id=1, source_target_pairs={{0,24},{8,0},{16,8},{24,16},{1,25},{9,1},{17,9},{25,17},{2,26},{10... | collective-permute-start | bytes 221192 | tf_op jit(solution)/shard_map/ppermute | solution.py:43
  184.0 7.9 %collective-permute-start.17 = (bf16[192,192]{0,1:T(8,128)(2,1)S(1)}, bf16[192,192]{0,1:T(8,128)(2,1)S(1)}, u32[]{:S(2)}, u32[]{:S(2)}) collective-permute-start(bf16[192,192]{0,1:T(8,128)(2,1)S(1)} %fusion.29), channel_id=1, source_target_pairs={{0,8},{8,16},{16,24},{24,0},{1,9},{9,17},{17,25},{25,1},{2,10},{10... | collective-permute-start | bytes 221192 | tf_op jit(solution)/shard_map/ppermute | solution.py:43
where the time goes:
time: 224 us; the launch traced here: 223 us
  starting transfers between devices  71.7 us (32%)
  blocking collectives  55.8 us (25%)
  waiting for transfers between devices  41.5 us (19%)
  local copies, waits for them, and re-layouts  23.1 us (10%)
  matrix products  19.5 us (9%)
  other arithmetic  9.77 us (4%)
    ppermute x17, starting transfers between devices, shift(): return lax.ppermute(x, self.axis, perm=pairs)  56.1 us
    ppermute x17, waiting for transfers between devices, shift(): return lax.ppermute(x, self.axis, perm=pairs)  38.6 us
    all_gather x1, blocking collectives, shards(): by_dp = lax.all_gather(over_seq, 'dp', axis=0, tiled=False)  18.7 us
    ppermute x2, starting transfers between devices, dp_partner(): return lax.ppermute(x, 'dp', perm=pairs)  15.6 us
    all_gather x1, blocking collectives, shards(): stack_y = lax.all_gather(w_mine, 'fh', axis=0, tiled=False)  13.7 us
    all_gather x1, blocking collectives, shards(): packed_all = lax.all_gather(packed, 'seq', axis=0, tiled=True)  12.4 us
    all_gather x1, blocking collectives, shards(): by_seq = lax.all_gather(over_fsdp, 'seq', axis=0, tiled=False)  11 us
    unnamed x23, local copies, waits for them, and re-layouts  9.48 us
  transfers between devices with their start and end apart: 19, of which 16 were waited for; matrix products, arithmetic and copies ran while one was open for 11% of the time, Pallas kernels for 0%

commit v1 on v0

--- a/solution.py
+++ b/solution.py
@@ -3,6 +3,28 @@
 import jax.numpy as jnp
 from jax import lax
 from jax.sharding import PartitionSpec as P
+
+
+def joined_along(blocks, dim):
+    shape = list(blocks.shape[1:])
+    shape[dim] *= blocks.shape[0]
+    return jnp.moveaxis(blocks, 0, dim).reshape(shape)
+
+
+def collect(x, axis, dim):
+    count = lax.axis_size(axis)
+    pairs = [(i, (i + 1) % count) for i in range(count)]
+    back = [(b, a) for a, b in pairs]
+    lower, upper = ([], [])
+    for step in range(count - 1):
+        if step % 2 == 0:
+            lower.append(lax.ppermute(lower[-1] if lower else x, axis, pairs))
+        else:
+            upper.append(lax.ppermute(upper[-1] if upper else x, axis, back))
+    blocks = jnp.stack([*lower[::-1], x, *upper])
+    shift = lax.axis_index(axis) - len(lower)
+    blocks = blocks[(jnp.arange(count) - shift) % count]
+    return joined_along(blocks, dim)
 
 
 def contract_first(left, right):
@@ -141,7 +163,7 @@
     me_x = ring_x.position()
     ids_col = jnp.broadcast_to(image_ids.astype(jnp.bfloat16)[:, None], (n_rows, width_head))
     packed = jnp.concatenate([heads, grad_out, ids_col], axis=1)
-    packed_all = lax.all_gather(packed, "seq", axis=0, tiled=True)
+    packed_all = collect(packed, "seq", 0)
     query_all = packed_all[:, :width_head]
     keys_all = packed_all[:, width_head : 2 * width_head]
     values_all = packed_all[:, 2 * width_head : 3 * width_head]

time: 224 us -> 248 us (1.11)
  the two profiles are of different devices: /device:TPU:75 before, /device:TPU:1 now
where the time goes in v1:
time: 248 us; the launch traced here: 247 us
  starting transfers between devices  81.6 us (33%)
  waiting for transfers between devices  51.1 us (21%)
  blocking collectives  43.3 us (17%)
  local copies, waits for them, and re-layouts  29.1 us (12%)
  matrix products  26.6 us (11%)
  other arithmetic  13.8 us (6%)
    ppermute x17, starting transfers between devices, shift(): return lax.ppermute(x, self.axis, perm=pairs)  58.5 us
    ppermute x17, waiting for transfers between devices, shift(): return lax.ppermute(x, self.axis, perm=pairs)  36.4 us
    all_gather x1, blocking collectives, shards(): by_dp = lax.all_gather(over_seq, 'dp', axis=0, tiled=False)  16.3 us
    all_gather x1, blocking collectives, shards(): stack_y = lax.all_gather(w_mine, 'fh', axis=0, tiled=False)  16.3 us
    ppermute x2, starting transfers between devices, dp_partner(): return lax.ppermute(x, 'dp', perm=pairs)  14.7 us
    ppermute x2, waiting for transfers between devices, collect(): lower.append(lax.ppermute(lower[-1] if lower else x, axis, pairs))  11.7 us
    unnamed x27, local copies, waits for them, and re-layouts  11.7 us
    all_gather x1, blocking collectives, shards(): by_seq = lax.all_gather(over_fsdp, 'seq', axis=0, tiled=False)  10.7 us
  transfers between devices with their start and end apart: 22, of which 18 were waited for; matrix products, arithmetic and copies ran while one was open for 10% of the time, Pallas kernels for 0%

profile of v1, /device:TPU:1, one launch (start us, length us, event | category | flops | bytes accessed | tf_op | source)
XLA Modules:
  0.0 246.8 jit_solution(13203423899966054638)
XLA Ops:
  1.6 16.3 %all-gather = bf16[768,192]{1,0:T(8,128)(2,1)S(1)} all-gather(bf16[192,192]{1,0:T(8,128)(2,1)S(1)} %constant_dynamic-slice_fusion), channel_id=2, replica_groups=mesh['dp'=4,'seq'=4,'fh'=4,'fz'=8] {'fh'}, dimensions={0}, use_global_device_ids=true | all-gather | bytes 368640 | tf_op jit(solution)/shard_map/all_gather | solution.py:143
  17.9 3.2 %collective-permute-start = (bf16[4,192,192]{2,1,0:T(8,128)(2,1)S(1)}, bf16[4,192,192]{2,1,0:T(8,128)(2,1)}, u32[]{:S(2)}, u32[]{:S(2)}) collective-permute-start(bf16[4,192,192]{2,1,0:T(8,128)(2,1)S(1)} %bitcast.124), channel_id=1, source_target_pairs={{0,1},{1,2},{2,3},{3,4},{4,5},{5,6},{6,7},{7,0},{8,9},{9,10},{10,1... | collective-permute-start | bytes 884744 | tf_op jit(solution)/shard_map/ppermute | solution.py:65
  21.2 8.6 %collective-permute-start.1 = (bf16[4,192,192]{2,1,0:T(8,128)(2,1)S(1)}, bf16[4,192,192]{2,1,0:T(8,128)(2,1)S(1)}, u32[]{:S(2)}, u32[]{:S(2)}) collective-permute-start(bf16[4,192,192]{2,1,0:T(8,128)(2,1)S(1)} %bitcast.125), channel_id=1, source_target_pairs={{0,7},{1,0},{2,1},{3,2},{4,3},{5,4},{6,5},{7,6},{8,15},{9,8},{10,9... | collective-permute-start | bytes 884744 | tf_op jit(solution)/shard_map/ppermute | solution.py:65
  30.6 1.5 gather_fusion
  33.1 1.9 collective-permute-start.2
  35.0 1.8 bitcast_dynamic-update-slice_fusion.6
  36.8 4.6 %collective-permute-start.3 = (bf16[4,192,192]{2,1,0:T(8,128)(2,1)S(1)}, bf16[4,192,192]{2,1,0:T(8,128)(2,1)S(1)}, u32[]{:S(2)}, u32[]{:S(2)}) collective-permute-start(bf16[4,192,192]{2,1,0:T(8,128)(2,1)S(1)} %collective-permute-done.1), channel_id=1, source_target_pairs={{0,7},{1,0},{2,1},{3,2},{4,3},{5,4},{6,5},{7,6},{8,15},{9,8},{10,9... | collective-permute-start | bytes 884744 | tf_op jit(solution)/shard_map/ppermute | solution.py:65
  43.0 1.9 collective-permute-start.4
  46.0 5.0 %collective-permute-start.5 = (bf16[4,192,192]{2,1,0:T(8,128)(2,1)S(1)}, bf16[4,192,192]{2,1,0:T(8,128)(2,1)S(1)}, u32[]{:S(2)}, u32[]{:S(2)}) collective-permute-start(bf16[4,192,192]{2,1,0:T(8,128)(2,1)S(1)} %collective-permute-done.3), channel_id=1, source_target_pairs={{0,7},{1,0},{2,1},{3,2},{4,3},{5,4},{6,5},{7,6},{8,15},{9,8},{10,9... | collective-permute-start | bytes 884744 | tf_op jit(solution)/shard_map/ppermute | solution.py:65
  51.8 1.2 collective-permute-done.4
  53.0 1.9 collective-permute-start.6
  55.0 1.8 bitcast_dynamic-update-slice_fusion.2
  56.8 4.5 %reshape.193 = bf16[192,4,8,192]{3,2,1,0:T(8,128)(2,1)} reshape(bf16[192,6144]{1,0:T(8,128)(2,1)S(1)} %bitcast.113) | data formatting | bytes 4718592 | tf_op jit(solution)/shard_map/reshape | solution.py:144
  62.1 2.0 collective-permute-done.6
  64.0 1.8 bitcast_dynamic-update-slice_fusion
  65.8 2.6 %gather_fusion.1 = bf16[32,192,192]{2,1,0:T(8,128)(2,1)S(1)} fusion(bf16[32,192,192]{2,1,0:T(8,128)(2,1)} %bitcast.114, s32[1024]{0:T(1024)S(1)} %pad_clamp_fusion.1), kind=kCustom, calls=%fused_computation.1 | custom fusion | bytes 4718720 | tf_op jit(solution)/shard_map/jit(_take)/gather | solution.py:151
  68.5 2.6 %copy.33 = bf16[6144,192]{0,1:T(8,128)(2,1)} copy(bf16[6144,192]{1,0:T(8,128)(2,1)S(1)} %bitcast.110) | data formatting | bytes 4718592 | tf_op jit(solution)/shard_map/reshape | solution.py:151
  71.1 10.5 %collective-permute-start.7 = (bf16[6144,192]{0,1:T(8,128)(2,1)}, bf16[6144,192]{0,1:T(8,128)(2,1)}, u32[]{:S(2)}, u32[]{:S(2)}) collective-permute-start(bf16[6144,192]{0,1:T(8,128)(2,1)} %copy.33), channel_id=1, source_target_pairs={{0,128},{128,0},{256,384},{384,256},{1,129},{129,1},{257,385},{385... | collective-permute-start | bytes 7077896 | tf_op jit(solution)/shard_map/ppermute | solution.py:44
  81.6 2.6 %convolution_bitcast_fusion.1 = bf16[192,192]{1,0:T(8,128)(2,1)S(1)} fusion(bf16[6144,192]{1,0:T(8,128)(2,1)S(1)} %bitcast.111, bf16[1,192,6144]{2,1,0:T(8,128)(2,1)} %param.5), kind=kOutput, calls=%fused_computation.22 | convolution fusion | flops 452984832 | bytes 4792320 | tf_op jit(solution)/shard_map/dot_general | solution.py:153
  84.2 1.8 collective-permute-done.7
  86.0 2.5 convolution_bitcast_fusion
  89.5 3.1 %collective-permute-start.8 = (bf16[192,640]{1,0:T(8,128)(2,1)}, bf16[192,640]{1,0:T(8,128)(2,1)}, u32[]{:S(2)}, u32[]{:S(2)}) collective-permute-start(bf16[192,640]{1,0:T(8,128)(2,1)} %get-tuple-element.33), channel_id=1, source_target_pairs={{0,32},{32,64},{64,96},{96,0},{1,33},{33,65},{65,97},{97,1},{2,34}... | collective-permute-start | bytes 737288 | tf_op jit(solution)/shard_map/ppermute | solution.py:21
  92.6 3.4 %collective-permute-start.10 = (bf16[192,640]{1,0:T(8,128)(2,1)}, bf16[192,640]{1,0:T(8,128)(2,1)}, u32[]{:S(2)}, u32[]{:S(2)}) collective-permute-start(bf16[192,640]{1,0:T(8,128)(2,1)} %get-tuple-element.33), channel_id=1, source_target_pairs={{32,0},{64,32},{96,64},{0,96},{33,1},{65,33},{97,65},{1,97},{34,2}... | collective-permute-start | bytes 737288 | tf_op jit(solution)/shard_map/ppermute | solution.py:23
  96.0 4.1 %collective-permute-done.8 = bf16[192,640]{1,0:T(8,128)(2,1)} collective-permute-done((bf16[192,640]{1,0:T(8,128)(2,1)}, bf16[192,640]{1,0:T(8,128)(2,1)}, u32[]{:S(2)}, u32[]{:S(2)}) %collective-permute-start.8) | collective-permute-done | bytes 245792 | tf_op jit(solution)/shard_map/ppermute | solution.py:21
  100.0 1.9 collective-permute-start.9
  102.0 7.7 %collective-permute-done.9 = bf16[192,640]{1,0:T(8,128)(2,1)} collective-permute-done((bf16[192,640]{1,0:T(8,128)(2,1)}, bf16[192,640]{1,0:T(8,128)(2,1)}, u32[]{:S(2)}, u32[]{:S(2)}) %collective-permute-start.9) | collective-permute-done | bytes 245792 | tf_op jit(solution)/shard_map/ppermute | solution.py:21
  109.7 2.3 pad_maximum_fusion
  112.0 2.8 %gather_fusion.2 = bf16[4,192,640]{2,1,0:T(8,128)(2,1)} fusion(bf16[4,192,640]{2,1,0:T(8,128)(2,1)} %pad_maximum_fusion, s32[1024]{0:T(1024)S(1)} %pad_clamp_fusion), kind=kCustom, calls=%fused_computation.2 | custom fusion | bytes 1966096 | tf_op jit(solution)/shard_map/gather | solution.py:26
  114.8 1.1 slice_reduce_fusion
  116.8 1.5 fusion.8
  119.8 1.5 fusion.12
  122.1 1.2 convolution_convert_fusion
  123.3 1.8 fusion.13
  125.1 2.9 %multiply_convert_fusion = bf16[768,768]{0,1:T(8,128)(2,1)S(1)} fusion(f32[768,768]{0,1:T(8,128)} %copy-done.6, f32[768]{0:T(1024)S(1)} %fusion.13, f32[768]{0:T(1024)S(1)} %log_add_fusion, bf16[768]{0:T(1024)(128)(2,1)S(1)} %slice_reduce_fusion, bf16[768,640]{1,0:T(8,128)(2,1)} %bitcast.120), kind=kOutput, calls=%fused_computation.17 | convolution fusion | flops 155713536 | bytes 3944448 | tf_op jit(solution)/shard_map/dot_general | solution.py:37
  128.0 1.4 convolution_convert_fusion.2
  129.4 1.2 convolution_convert_fusion.1
  130.5 4.1 %convert_bitcast_fusion = bf16[8,4,192,192]{2,3,0,1:T(8,128)(2,1)} fusion(bf16[192,4,8,192]{3,2,1,0:T(8,128)(2,1)S(1)} %copy-done.1, pred[]{:T(512)S(6)} %eq.41, bf16[192,128]{1,0:T(8,128)(2,1)S(1)} %convolution_convert_fusion.1, bf16[192,128]{1,0:T(8,128)(2,1)S(1)} %convolution_convert_fusion.2, bf16[192,128]{1,0:T(8,128)(2,1)S(1)} %convolution_convert_fusion), kind=kOutput, calls=%fused_computation.9 | convolution fusion | flops 454496256 | bytes 4866049 | tf_op jit(solution)/shard_map/pyzd,pc->zydc/dot_general | solution.py:198
  134.7 4.2 %collective-permute-start.11 = (bf16[8,4,192,192]{2,3,0,1:T(8,128)(2,1)}, bf16[8,4,192,192]{2,3,0,1:T(8,128)(2,1)}, u32[]{:S(2)}, u32[]{:S(2)}) collective-permute-start(bf16[8,4,192,192]{2,3,0,1:T(8,128)(2,1)} %convert_bitcast_fusion), channel_id=1, source_target_pairs={{0,128},{128,0},{256,384},{384,256},{1,129},{129,1},{257,385},{385... | collective-permute-start | bytes 7077896 | tf_op jit(solution)/shard_map/ppermute | solution.py:44
  139.0 1.2 fusion.54
  140.8 2.4 fusion.5
  144.3 3.0 %convert_add_fusion = f32[8,4,192,192]{2,3,0,1:T(8,128)S(1)} fusion(f32[8,4,192,192]{2,3,0,1:T(8,128)S(1)} %fusion.5, bf16[8,4,192,192]{2,3,0,1:T(8,128)(2,1)} %collective-permute-done.11), kind=kLoop, calls=%fused_computation.5 | loop fusion | flops 2359296 | bytes 11796480 | tf_op jit(solution)/shard_map/add | solution.py:202
  147.5 1.9 collective-permute-start.12
  149.4 4.0 %fusion = bf16[192,6144]{1,0:T(8,128)(2,1)} fusion(f32[192,6144]{1,0:T(8,128)S(1)} %fusion.54, bf16[6144,192]{0,1:T(8,128)(2,1)} %collective-permute-done.7, pred[]{:T(512)S(6)} %eq.41, bf16[192,128]{1,0:T(8,128)(2,1)S(1)} %convolution_convert_fusion.1, bf16[192,128]{1,0:T(8,128)(2,1)S(1)} %convolution_convert_fusion.2, ...), kind=kOutput, calls=%fused_computation.4 | convolution fusion | flops 455675904 | bytes 9584641 | tf_op jit(solution)/shard_map/dot_general | solution.py:37
  153.3 4.5 %collective-permute-start.16 = (bf16[4,192,192]{1,2,0:T(8,128)(2,1)S(1)}, bf16[4,192,192]{1,2,0:T(8,128)(2,1)S(1)}, u32[]{:S(2)}, u32[]{:S(2)}) collective-permute-start(bf16[4,192,192]{1,2,0:T(8,128)(2,1)S(1)} %get-tuple-element.26), channel_id=1, source_target_pairs={{0,7},{1,0},{2,1},{3,2},{4,3},{5,4},{6,5},{7,6},{8,15},{9,8},{10,9... | collective-permute-start | bytes 884744 | tf_op jit(solution)/shard_map/ppermute | solution.py:65
  157.9 3.0 %collective-permute-done.12 = bf16[4,192,192]{1,2,0:T(8,128)(2,1)S(1)} collective-permute-done((bf16[4,192,192]{1,2,0:T(8,128)(2,1)S(1)}, bf16[4,192,192]{1,2,0:T(8,128)(2,1)S(1)}, u32[]{:S(2)}, u32[]{:S(2)}) %collective-permute-start.12) | collective-permute-done | bytes 294944 | tf_op jit(solution)/shard_map/ppermute | solution.py:65
  161.0 1.9 collective-permute-start.13
  163.0 2.7 %collective-permute-done.16 = bf16[4,192,192]{1,2,0:T(8,128)(2,1)S(1)} collective-permute-done((bf16[4,192,192]{1,2,0:T(8,128)(2,1)S(1)}, bf16[4,192,192]{1,2,0:T(8,128)(2,1)S(1)}, u32[]{:S(2)}, u32[]{:S(2)}) %collective-permute-start.16) | collective-permute-done | bytes 294944 | tf_op jit(solution)/shard_map/ppermute | solution.py:65
  165.6 7.9 %collective-permute-done.13 = bf16[4,192,192]{1,2,0:T(8,128)(2,1)S(1)} collective-permute-done((bf16[4,192,192]{1,2,0:T(8,128)(2,1)S(1)}, bf16[4,192,192]{1,2,0:T(8,128)(2,1)S(1)}, u32[]{:S(2)}, u32[]{:S(2)}) %collective-permute-start.13) | collective-permute-done | bytes 294944 | tf_op jit(solution)/shard_map/ppermute | solution.py:65
  173.5 1.6 fusion.17
  175.1 1.9 collective-permute-start.14
  177.0 4.6 %collective-permute-start.17 = (bf16[4,192,192]{1,2,0:T(8,128)(2,1)S(1)}, bf16[4,192,192]{1,2,0:T(8,128)(2,1)S(1)}, u32[]{:S(2)}, u32[]{:S(2)}) collective-permute-start(bf16[4,192,192]{1,2,0:T(8,128)(2,1)S(1)} %get-tuple-element.25), channel_id=1, source_target_pairs={{0,7},{1,0},{2,1},{3,2},{4,3},{5,4},{6,5},{7,6},{8,15},{9,8},{10,9... | collective-permute-start | bytes 884744 | tf_op jit(solution)/shard_map/ppermute | solution.py:65
  181.6 5.0 %collective-permute-done.14 = bf16[4,192,192]{1,2,0:T(8,128)(2,1)S(1)} collective-permute-done((bf16[4,192,192]{1,2,0:T(8,128)(2,1)S(1)}, bf16[4,192,192]{1,2,0:T(8,128)(2,1)S(1)}, u32[]{:S(2)}, u32[]{:S(2)}) %collective-permute-start.14) | collective-permute-done | bytes 294944 | tf_op jit(solution)/shard_map/ppermute | solution.py:65
  187.5 1.6 fusion.16
  189.1 1.9 collective-permute-start.15
  191.0 5.3 %collective-permute-start.18 = (bf16[4,192,192]{1,2,0:T(8,128)(2,1)S(1)}, bf16[4,192,192]{1,2,0:T(8,128)(2,1)S(1)}, u32[]{:S(2)}, u32[]{:S(2)}) collective-permute-start(bf16[4,192,192]{1,2,0:T(8,128)(2,1)S(1)} %get-tuple-element.23), channel_id=1, source_target_pairs={{0,7},{1,0},{2,1},{3,2},{4,3},{5,4},{6,5},{7,6},{8,15},{9,8},{10,9... | collective-permute-start | bytes 884744 | tf_op jit(solution)/shard_map/ppermute | solution.py:65
  196.4 4.1 %collective-permute-done.15 = bf16[4,192,192]{1,2,0:T(8,128)(2,1)S(1)} collective-permute-done((bf16[4,192,192]{1,2,0:T(8,128)(2,1)S(1)}, bf16[4,192,192]{1,2,0:T(8,128)(2,1)S(1)}, u32[]{:S(2)}, u32[]{:S(2)}) %collective-permute-start.15) | collective-permute-done | bytes 294944 | tf_op jit(solution)/shard_map/ppermute | solution.py:65
  200.5 1.2 collective-permute-done.18
  201.7 1.2 fusion.19
  203.0 1.9 collective-permute-start.19
  205.0 5.5 %collective-permute-start.21 = (bf16[192,192]{0,1:T(8,128)(2,1)S(1)}, bf16[192,192]{0,1:T(8,128)(2,1)S(1)}, u32[]{:S(2)}, u32[]{:S(2)}) collective-permute-start(bf16[192,192]{0,1:T(8,128)(2,1)S(1)} %get-tuple-element.31), channel_id=1, source_target_pairs={{0,24},{8,0},{16,8},{24,16},{1,25},{9,1},{17,9},{25,17},{2,26},{10... | collective-permute-start | bytes 221192 | tf_op jit(solution)/shard_map/ppermute | solution.py:65
  211.2 1.9 collective-permute-start.20
  213.2 5.5 %collective-permute-done.20 = bf16[192,192]{0,1:T(8,128)(2,1)S(1)} collective-permute-done((bf16[192,192]{0,1:T(8,128)(2,1)S(1)}, bf16[192,192]{0,1:T(8,128)(2,1)S(1)}, u32[]{:S(2)}, u32[]{:S(2)}) %collective-permute-start.20) | collective-permute-done | bytes 73760 | tf_op jit(solution)/shard_map/ppermute | solution.py:65
  218.9 10.7 %all-gather.1 = f32[768,192]{1,0:T(8,128)S(1)} all-gather(f32[192,192]{1,0:T(8,128)S(1)} %copy.42), channel_id=3, replica_groups=mesh['dp'=4,'seq'=4,'fh'=4,'fz'=8] {'seq'}, dimensions={0}, use_global_device_ids=true | all-gather | bytes 737280 | tf_op jit(solution)/shard_map/all_gather | solution.py:205
  229.6 16.3 %all_gather.20 = f32[4,192,192]{2,1,0:T(8,128)S(1)} all-gather(f32[1,192,192]{2,1,0:T(8,128)S(1)} %fusion.28), channel_id=1, replica_groups=mesh['dp'=4,'seq'=4,'fh'=4,'fz'=8] {'dp'}, dimensions={0}, use_global_device_ids=true | all-gather | bytes 737280 | tf_op jit(solution)/shard_map/all_gather | solution.py:209
  (57 shorter events, 16.1 us)
Async XLA Ops:
  0.6 0.9 copy-start
  17.9 15.2 %collective-permute-start = (bf16[4,192,192]{2,1,0:T(8,128)(2,1)S(1)}, bf16[4,192,192]{2,1,0:T(8,128)(2,1)}, u32[]{:S(2)}, u32[]{:S(2)}) collective-permute-start(bf16[4,192,192]{2,1,0:T(8,128)(2,1)S(1)} %bitcast.124), channel_id=1, source_target_pairs={{0,1},{1,2},{2,3},{3,4},{4,5},{5,6},{6,7},{7,0},{8,9},{9,10},{10,1... | collective-permute-start | bytes 884744 | tf_op jit(solution)/shard_map/ppermute | solution.py:65
  21.2 15.6 %collective-permute-start.1 = (bf16[4,192,192]{2,1,0:T(8,128)(2,1)S(1)}, bf16[4,192,192]{2,1,0:T(8,128)(2,1)S(1)}, u32[]{:S(2)}, u32[]{:S(2)}) collective-permute-start(bf16[4,192,192]{2,1,0:T(8,128)(2,1)S(1)} %bitcast.125), channel_id=1, source_target_pairs={{0,7},{1,0},{2,1},{3,2},{4,3},{5,4},{6,5},{7,6},{8,15},{9,8},{10,9... | collective-permute-start | bytes 884744 | tf_op jit(solution)/shard_map/ppermute | solution.py:65
  30.5 26.2 %copy-start.4 = (bf16[1,192,6144]{2,1,0:T(8,128)(2,1)S(1)}, bf16[1,192,6144]{2,1,0:T(8,128)(2,1)}, u32[]{:S(2)}) copy-start(bf16[1,192,6144]{2,1,0:T(8,128)(2,1)} %param.5) | copy-start | bytes 7077892
  33.1 9.9 %collective-permute-start.2 = (bf16[4,192,192]{2,1,0:T(8,128)(2,1)}, bf16[4,192,192]{2,1,0:T(8,128)(2,1)S(1)}, u32[]{:S(2)}, u32[]{:S(2)}) collective-permute-start(bf16[4,192,192]{2,1,0:T(8,128)(2,1)} %collective-permute-done), channel_id=1, source_target_pairs={{0,1},{1,2},{2,3},{3,4},{4,5},{5,6},{6,7},{7,0},{8,9},{9,10},{10,1... | collective-permute-start | bytes 884744 | tf_op jit(solution)/shard_map/ppermute | solution.py:65
  36.8 9.3 %collective-permute-start.3 = (bf16[4,192,192]{2,1,0:T(8,128)(2,1)S(1)}, bf16[4,192,192]{2,1,0:T(8,128)(2,1)S(1)}, u32[]{:S(2)}, u32[]{:S(2)}) collective-permute-start(bf16[4,192,192]{2,1,0:T(8,128)(2,1)S(1)} %collective-permute-done.1), channel_id=1, source_target_pairs={{0,7},{1,0},{2,1},{3,2},{4,3},{5,4},{6,5},{7,6},{8,15},{9,8},{10,9... | collective-permute-start | bytes 884744 | tf_op jit(solution)/shard_map/ppermute | solution.py:65
  43.0 10.0 %collective-permute-start.4 = (bf16[4,192,192]{2,1,0:T(8,128)(2,1)S(1)}, bf16[4,192,192]{2,1,0:T(8,128)(2,1)}, u32[]{:S(2)}, u32[]{:S(2)}) collective-permute-start(bf16[4,192,192]{2,1,0:T(8,128)(2,1)S(1)} %collective-permute-done.2), channel_id=1, source_target_pairs={{0,1},{1,2},{2,3},{3,4},{4,5},{5,6},{6,7},{7,0},{8,9},{9,10},{10,1... | collective-permute-start | bytes 884744 | tf_op jit(solution)/shard_map/ppermute | solution.py:65
  46.0 10.7 %collective-permute-start.5 = (bf16[4,192,192]{2,1,0:T(8,128)(2,1)S(1)}, bf16[4,192,192]{2,1,0:T(8,128)(2,1)S(1)}, u32[]{:S(2)}, u32[]{:S(2)}) collective-permute-start(bf16[4,192,192]{2,1,0:T(8,128)(2,1)S(1)} %collective-permute-done.3), channel_id=1, source_target_pairs={{0,7},{1,0},{2,1},{3,2},{4,3},{5,4},{6,5},{7,6},{8,15},{9,8},{10,9... | collective-permute-start | bytes 884744 | tf_op jit(solution)/shard_map/ppermute | solution.py:65
  53.0 11.0 %collective-permute-start.6 = (bf16[4,192,192]{2,1,0:T(8,128)(2,1)}, bf16[4,192,192]{2,1,0:T(8,128)(2,1)}, u32[]{:S(2)}, u32[]{:S(2)}) collective-permute-start(bf16[4,192,192]{2,1,0:T(8,128)(2,1)} %collective-permute-done.4), channel_id=1, source_target_pairs={{0,1},{1,2},{2,3},{3,4},{4,5},{5,6},{6,7},{7,0},{8,9},{9,10},{10,1... | collective-permute-start | bytes 884744 | tf_op jit(solution)/shard_map/ppermute | solution.py:65
  68.5 13.1 %copy-start.8 = (s32[1,192]{1,0:T(1,128)S(1)}, s32[1,192]{1,0:T(1,128)}, u32[]{:S(2)}) copy-start(s32[1,192]{1,0:T(1,128)} %param.6) | copy-start | bytes 2308
  71.1 14.9 %collective-permute-start.7 = (bf16[6144,192]{0,1:T(8,128)(2,1)}, bf16[6144,192]{0,1:T(8,128)(2,1)}, u32[]{:S(2)}, u32[]{:S(2)}) collective-permute-start(bf16[6144,192]{0,1:T(8,128)(2,1)} %copy.33), channel_id=1, source_target_pairs={{0,128},{128,0},{256,384},{384,256},{1,129},{129,1},{257,385},{385... | collective-permute-start | bytes 7077896 | tf_op jit(solution)/shard_map/ppermute | solution.py:44
  81.6 4.4 %copy-start.5 = (bf16[1,192,6144]{2,1,0:T(8,128)(2,1)S(1)}, bf16[1,192,6144]{2,1,0:T(8,128)(2,1)}, u32[]{:S(2)}) copy-start(bf16[1,192,6144]{2,1,0:T(8,128)(2,1)} %param.5) | copy-start | bytes 7077892
  84.2 4.5 %copy-start.7 = (bf16[1,192,128]{2,1,0:T(8,128)(2,1)S(1)}, bf16[1,192,128]{2,1,0:T(8,128)(2,1)}, u32[]{:S(2)}) copy-start(bf16[1,192,128]{2,1,0:T(8,128)(2,1)} %param.8) | copy-start | bytes 147460
  89.5 10.6 %collective-permute-start.8 = (bf16[192,640]{1,0:T(8,128)(2,1)}, bf16[192,640]{1,0:T(8,128)(2,1)}, u32[]{:S(2)}, u32[]{:S(2)}) collective-permute-start(bf16[192,640]{1,0:T(8,128)(2,1)} %get-tuple-element.33), channel_id=1, source_target_pairs={{0,32},{32,64},{64,96},{96,0},{1,33},{33,65},{65,97},{97,1},{2,34}... | collective-permute-start | bytes 737288 | tf_op jit(solution)/shard_map/ppermute | solution.py:21
  92.6 9.4 %collective-permute-start.10 = (bf16[192,640]{1,0:T(8,128)(2,1)}, bf16[192,640]{1,0:T(8,128)(2,1)}, u32[]{:S(2)}, u32[]{:S(2)}) collective-permute-start(bf16[192,640]{1,0:T(8,128)(2,1)} %get-tuple-element.33), channel_id=1, source_target_pairs={{32,0},{64,32},{96,64},{0,96},{33,1},{65,33},{97,65},{1,97},{34,2}... | collective-permute-start | bytes 737288 | tf_op jit(solution)/shard_map/ppermute | solution.py:23
  100.0 9.7 %collective-permute-start.9 = (bf16[192,640]{1,0:T(8,128)(2,1)}, bf16[192,640]{1,0:T(8,128)(2,1)}, u32[]{:S(2)}, u32[]{:S(2)}) collective-permute-start(bf16[192,640]{1,0:T(8,128)(2,1)} %collective-permute-done.8), channel_id=1, source_target_pairs={{0,32},{32,64},{64,96},{96,0},{1,33},{33,65},{65,97},{97,1},{2,34}... | collective-permute-start | bytes 737288 | tf_op jit(solution)/shard_map/ppermute | solution.py:21
  118.3 1.4 copy-start.6
  125.1 5.4 %copy-start.1 = (bf16[192,4,8,192]{3,2,1,0:T(8,128)(2,1)S(1)}, bf16[192,4,8,192]{3,2,1,0:T(8,128)(2,1)}, u32[]{:S(2)}) copy-start(bf16[192,4,8,192]{3,2,1,0:T(8,128)(2,1)} %reshape.193) | copy-start | bytes 7077892
  134.7 9.7 %collective-permute-start.11 = (bf16[8,4,192,192]{2,3,0,1:T(8,128)(2,1)}, bf16[8,4,192,192]{2,3,0,1:T(8,128)(2,1)}, u32[]{:S(2)}, u32[]{:S(2)}) collective-permute-start(bf16[8,4,192,192]{2,3,0,1:T(8,128)(2,1)} %convert_bitcast_fusion), channel_id=1, source_target_pairs={{0,128},{128,0},{256,384},{384,256},{1,129},{129,1},{257,385},{385... | collective-permute-start | bytes 7077896 | tf_op jit(solution)/shard_map/ppermute | solution.py:44
  138.9 1.9 copy-start.2
  147.3 13.5 %copy-start.3 = (f32[8,4,192,192]{2,3,0,1:T(8,128)}, f32[8,4,192,192]{2,3,0,1:T(8,128)S(1)}, u32[]{:S(2)}) copy-start(f32[8,4,192,192]{2,3,0,1:T(8,128)S(1)} %convert_add_fusion) | copy-start | bytes 14155780
  147.5 13.4 %collective-permute-start.12 = (bf16[4,192,192]{1,2,0:T(8,128)(2,1)S(1)}, bf16[4,192,192]{1,2,0:T(8,128)(2,1)S(1)}, u32[]{:S(2)}, u32[]{:S(2)}) collective-permute-start(bf16[4,192,192]{1,2,0:T(8,128)(2,1)S(1)} %get-tuple-element.27), channel_id=1, source_target_pairs={{0,1},{1,2},{2,3},{3,4},{4,5},{5,6},{6,7},{7,0},{8,9},{9,10},{10,1... | collective-permute-start | bytes 884744 | tf_op jit(solution)/shard_map/ppermute | solution.py:65
  153.3 12.3 %collective-permute-start.16 = (bf16[4,192,192]{1,2,0:T(8,128)(2,1)S(1)}, bf16[4,192,192]{1,2,0:T(8,128)(2,1)S(1)}, u32[]{:S(2)}, u32[]{:S(2)}) collective-permute-start(bf16[4,192,192]{1,2,0:T(8,128)(2,1)S(1)} %get-tuple-element.26), channel_id=1, source_target_pairs={{0,7},{1,0},{2,1},{3,2},{4,3},{5,4},{6,5},{7,6},{8,15},{9,8},{10,9... | collective-permute-start | bytes 884744 | tf_op jit(solution)/shard_map/ppermute | solution.py:65
  161.0 12.5 %collective-permute-start.13 = (bf16[4,192,192]{1,2,0:T(8,128)(2,1)S(1)}, bf16[4,192,192]{1,2,0:T(8,128)(2,1)S(1)}, u32[]{:S(2)}, u32[]{:S(2)}) collective-permute-start(bf16[4,192,192]{1,2,0:T(8,128)(2,1)S(1)} %fusion.18), channel_id=1, source_target_pairs={{0,1},{1,2},{2,3},{3,4},{4,5},{5,6},{6,7},{7,0},{8,9},{9,10},{10,1... | collective-permute-start | bytes 884744 | tf_op jit(solution)/shard_map/ppermute | solution.py:65
  175.1 11.6 %collective-permute-start.14 = (bf16[4,192,192]{1,2,0:T(8,128)(2,1)S(1)}, bf16[4,192,192]{1,2,0:T(8,128)(2,1)S(1)}, u32[]{:S(2)}, u32[]{:S(2)}) collective-permute-start(bf16[4,192,192]{1,2,0:T(8,128)(2,1)S(1)} %get-tuple-element.24), channel_id=1, source_target_pairs={{0,1},{1,2},{2,3},{3,4},{4,5},{5,6},{6,7},{7,0},{8,9},{9,10},{10,1... | collective-permute-start | bytes 884744 | tf_op jit(solution)/shard_map/ppermute | solution.py:65
  177.0 10.6 %collective-permute-start.17 = (bf16[4,192,192]{1,2,0:T(8,128)(2,1)S(1)}, bf16[4,192,192]{1,2,0:T(8,128)(2,1)S(1)}, u32[]{:S(2)}, u32[]{:S(2)}) collective-permute-start(bf16[4,192,192]{1,2,0:T(8,128)(2,1)S(1)} %get-tuple-element.25), channel_id=1, source_target_pairs={{0,7},{1,0},{2,1},{3,2},{4,3},{5,4},{6,5},{7,6},{8,15},{9,8},{10,9... | collective-permute-start | bytes 884744 | tf_op jit(solution)/shard_map/ppermute | solution.py:65
  189.1 11.4 %collective-permute-start.15 = (bf16[4,192,192]{1,2,0:T(8,128)(2,1)S(1)}, bf16[4,192,192]{1,2,0:T(8,128)(2,1)S(1)}, u32[]{:S(2)}, u32[]{:S(2)}) collective-permute-start(bf16[4,192,192]{1,2,0:T(8,128)(2,1)S(1)} %get-tuple-element.22), channel_id=1, source_target_pairs={{0,1},{1,2},{2,3},{3,4},{4,5},{5,6},{6,7},{7,0},{8,9},{9,10},{10,1... | collective-permute-start | bytes 884744 | tf_op jit(solution)/shard_map/ppermute | solution.py:65
  191.0 10.7 %collective-permute-start.18 = (bf16[4,192,192]{1,2,0:T(8,128)(2,1)S(1)}, bf16[4,192,192]{1,2,0:T(8,128)(2,1)S(1)}, u32[]{:S(2)}, u32[]{:S(2)}) collective-permute-start(bf16[4,192,192]{1,2,0:T(8,128)(2,1)S(1)} %get-tuple-element.23), channel_id=1, source_target_pairs={{0,7},{1,0},{2,1},{3,2},{4,3},{5,4},{6,5},{7,6},{8,15},{9,8},{10,9... | collective-permute-start | bytes 884744 | tf_op jit(solution)/shard_map/ppermute | solution.py:65
  203.0 8.2 %collective-permute-start.19 = (bf16[192,192]{0,1:T(8,128)(2,1)S(1)}, bf16[192,192]{0,1:T(8,128)(2,1)S(1)}, u32[]{:S(2)}, u32[]{:S(2)}) collective-permute-start(bf16[192,192]{0,1:T(8,128)(2,1)S(1)} %get-tuple-element.30), channel_id=1, source_target_pairs={{0,8},{8,16},{16,24},{24,0},{1,9},{9,17},{17,25},{25,1},{2,10},{10... | collective-permute-start | bytes 221192 | tf_op jit(solution)/shard_map/ppermute | solution.py:65
  205.0 8.2 %collective-permute-start.21 = (bf16[192,192]{0,1:T(8,128)(2,1)S(1)}, bf16[192,192]{0,1:T(8,128)(2,1)S(1)}, u32[]{:S(2)}, u32[]{:S(2)}) collective-permute-start(bf16[192,192]{0,1:T(8,128)(2,1)S(1)} %get-tuple-element.31), channel_id=1, source_target_pairs={{0,24},{8,0},{16,8},{24,16},{1,25},{9,1},{17,9},{25,17},{2,26},{10... | collective-permute-start | bytes 221192 | tf_op jit(solution)/shard_map/ppermute | solution.py:65
  211.2 7.5 %collective-permute-start.20 = (bf16[192,192]{0,1:T(8,128)(2,1)S(1)}, bf16[192,192]{0,1:T(8,128)(2,1)S(1)}, u32[]{:S(2)}, u32[]{:S(2)}) collective-permute-start(bf16[192,192]{0,1:T(8,128)(2,1)S(1)} %fusion.29), channel_id=1, source_target_pairs={{0,8},{8,16},{16,24},{24,0},{1,9},{9,17},{17,25},{25,1},{2,10},{10... | collective-permute-start | bytes 221192 | tf_op jit(solution)/shard_map/ppermute | solution.py:65
